TPU v7x, 32 devices: a whole 2x2x4 slice. The times are simulated.
32 devices in a mesh: row: 4 (over y, core), col: 8 (over z, x).
Axes of the slice: x: 2, y: 2, z: 4, core: 2. Of those that a mesh axis runs over, the one named last changes fastest.
Arguments:
- tokens: bfloat16 [512, 16384], P('col', 'row'), may hold values from -6 to 6
- gate_packed: bfloat16 [2560, 1024, 128], P('row', 'col'), may hold values from -0.0625 to 0.0625
- up_packed: bfloat16 [2560, 1024, 128], P('row', 'col'), may hold values from -0.0625 to 0.0625
- down_packed: bfloat16 [5120, 512, 128], P('col', 'row'), may hold values from -0.0546875 to 0.0546875
- gate_keep: int32 [128, 208], P('row', 'col'), may hold values from 0 to 1, as said below
- down_keep: int32 [208, 128], P('col', 'row'), may hold values from 0 to 1, as said below
Outputs:
- mixed: bfloat16 [512, 16384], P('col', 'row')
Inputs may be any that keep to these rules, and one draw needn't show every extreme that they name: `gate_keep`: in every tile of 32 x 26 blocks, at least 160 and at most 640 blocks are kept; some tile keeps exactly 640. `down_keep`: in every tile of 26 x 32 blocks, at least 160 and at most 640 blocks are kept; some tile keeps exactly 640.
All inputs are finite; a program needn't handle non-finite values.
Results may differ from a plain program's by a relative error of at most 0.02.
Values may be sent and summed in bfloat16 or wider, within the bound.
No kernel may reach another device: no remote copies, remote signals or barrier semaphores. Data moves between devices by JAX's collectives and lax.ppermute only.
A program may use at most 320 MiB of HBM per device.

v0:
```python
import jax
import jax.numpy as jnp
from jax import lax
from jax.sharding import PartitionSpec as P


def dense_tile(packed_tile, keep_tile):
    in_blocks, out_blocks = keep_tile.shape
    block = packed_tile.shape[2]
    flattened = keep_tile.reshape(-1)
    position = jnp.cumsum(flattened) - 1
    slot_index = jnp.where(flattened == 1, position, 0)
    picked = (
        jnp.take(packed_tile, slot_index, axis=0)
        * flattened.astype(packed_tile.dtype)[:, None, None]
    )
    picked = picked.reshape(in_blocks, out_blocks, block, block).transpose(0, 2, 1, 3)
    return picked.reshape(in_blocks * block, out_blocks * block)


def local(tokens, gate_packed, up_packed, down_packed, gate_keep, down_keep):
    gate_dense = dense_tile(gate_packed, gate_keep)
    up_dense = dense_tile(up_packed, gate_keep)
    down_dense = dense_tile(down_packed, down_keep)
    segment = lax.all_gather(tokens, "col", axis=0, tiled=True)
    gate_rows = jnp.dot(segment, gate_dense, preferred_element_type=jnp.float32)
    up_rows = jnp.dot(segment, up_dense, preferred_element_type=jnp.float32)
    gate_sum, up_sum = (
        lax.psum(gate_rows.astype(jnp.bfloat16), "row").astype(jnp.float32),
        lax.psum(up_rows.astype(jnp.bfloat16), "row").astype(jnp.float32),
    )
    every_hidden = (jax.nn.silu(gate_sum) * up_sum).astype(jnp.bfloat16)
    partial_out = jnp.dot(every_hidden, down_dense, preferred_element_type=jnp.float32)
    summed = lax.psum_scatter(
        partial_out.astype(jnp.bfloat16), "col", scatter_dimension=0, tiled=True
    )
    return summed


def solution(mesh):
    in_specs = (
        P("col", "row"),
        P("row", "col", None),
        P("row", "col", None),
        P("col", "row", None),
        P("row", "col"),
        P("col", "row"),
    )
    out_specs = P("col", "row")
    return jax.shard_map(local, mesh=mesh, in_specs=in_specs, out_specs=out_specs, check_vma=False)
```

profile of v0, /device:TPU:0, one launch (start us, length us, event | category | flops | bytes accessed | tf_op | source)
XLA Modules:
  0.0 473.7 jit_solution(3464177804756279992)
XLA Ops:
  6.5 0.0 all-gather.2.cloned.1.call-start
  6.5 0.7 all-gather.2.cloned.1.call-update
  7.3 0.0 all-reduce.5.cloned.1.call-start
  7.3 0.8 reshape.68
  8.1 0.3 reduce-window.16
  8.4 0.1 slice.20
  8.5 0.1 slice_reduce_fusion.1
  8.6 0.1 add_bitcast_fusion.1
  8.7 28.1 %gather_fusion = bf16[832,128,128]{2,1,0:T(8,128)(2,1)} fusion(bf16[640,128,128]{2,1,0:T(8,128)(2,1)} %param.9, s32[1024]{0:T(1024)S(1)} %pad_clamp_fusion.1), kind=kCustom, calls=%fused_computation.clone | custom fusion | bytes 54529280 | tf_op jit(solution)/shard_map/jit(_take)/gather | solution.py:14
  36.9 28.2 %gather_fusion.1 = bf16[832,128,128]{2,1,0:T(8,128)(2,1)} fusion(bf16[640,128,128]{2,1,0:T(8,128)(2,1)} %param.10, s32[1024]{0:T(1024)S(1)} %pad_clamp_fusion.1), kind=kCustom, calls=%fused_computation.1.clone | custom fusion | bytes 54529280 | tf_op jit(solution)/shard_map/jit(_take)/gather | solution.py:14
  65.1 36.6 %select_multiply_fusion.2 = (bf16[832,128,128]{2,1,0:T(8,128)(2,1)}, bf16[832,128,128]{2,1,0:T(8,128)(2,1)}) fusion(bf16[832,128,128]{2,1,0:T(8,128)(2,1)} %gather_fusion, pred[832]{0:T(1024)(128)(4,1)S(1)} %get-tuple-element.8, bf16[832]{0:T(1024)(128)(2,1)S(1)} %convert_element_type.39, bf16[832,128,128]{2,1,0:T(8,128)(2,1)} %gather_fusion.1), kind=kLoop, calls=%fused_computation.14 | loop fusion | flops 54525952 | bytes 109054400 | tf_op jit(solution)/shard_map/mul | solution.py:14
  101.7 35.0 %copy.8 = bf16[32,26,128,128]{2,0,3,1:T(8,128)(2,1)} copy(bf16[32,26,128,128]{3,2,1,0:T(8,128)(2,1)} %bitcast.51) | data formatting | bytes 54525952 | tf_op jit(solution)/shard_map/reshape | solution.py:17
  136.6 0.0 copy-start
  136.6 35.4 %copy.7 = bf16[32,26,128,128]{2,0,3,1:T(8,128)(2,1)} copy(bf16[32,26,128,128]{3,2,1,0:T(8,128)(2,1)} %bitcast.50) | data formatting | bytes 54525952 | tf_op jit(solution)/shard_map/reshape | solution.py:17
  172.0 0.0 copy-done
  172.0 0.1 reshape.75
  172.1 0.3 reduce-window.24
  172.4 0.1 slice.23
  172.5 0.0 all-gather.2.cloned.1.call-done
  172.5 24.4 %fusion.23 = bf16[512,3328]{0,1:T(8,128)(2,1)} fusion(bf16[512,4096]{1,0:T(8,128)(2,1)} %all-gather.2.cloned.1.call-done, bf16[416,8,32,128]{3,2,1,0:T(8,128)(2,1)} %bitcast.52), kind=kOutput, calls=%fused_computation.25 | convolution fusion | flops 13960347648 | bytes 34865152 | tf_op jit(solution)/shard_map/dot_general | solution.py:27
  197.0 24.5 %fusion.26 = bf16[512,3328]{0,1:T(8,128)(2,1)} fusion(bf16[512,4096]{1,0:T(8,128)(2,1)} %all-gather.2.cloned.1.call-done, bf16[416,8,32,128]{3,2,1,0:T(8,128)(2,1)} %bitcast.53), kind=kOutput, calls=%fused_computation.26 | convolution fusion | flops 13960347648 | bytes 34865152 | tf_op jit(solution)/shard_map/dot_general | solution.py:26
  221.5 0.0 all-reduce.5.cloned.1.call-update
  221.5 0.0 reduce-scatter.2.cloned.1.call-start
  221.5 0.1 slice_reduce_fusion
  221.7 0.1 add_bitcast_fusion
  221.7 27.2 %gather_fusion.2 = bf16[832,128,128]{2,1,0:T(8,128)(2,1)} fusion(bf16[640,128,128]{2,1,0:T(8,128)(2,1)} %param.11, s32[1024]{0:T(1024)S(1)} %pad_clamp_fusion), kind=kCustom, calls=%fused_computation.2.clone | custom fusion | bytes 54529280 | tf_op jit(solution)/shard_map/jit(_take)/gather | solution.py:14
  249.0 18.4 %select_multiply_fusion = bf16[832,128,128]{2,1,0:T(8,128)(2,1)} fusion(bf16[832,128,128]{2,1,0:T(8,128)(2,1)} %gather_fusion.2, pred[832]{0:T(1024)(128)(4,1)S(1)} %get-tuple-element.10, bf16[832]{0:T(1024)(128)(2,1)S(1)} %convert_element_type.47), kind=kLoop, calls=%fused_computation.12 | loop fusion | flops 27262976 | bytes 54528448 | tf_op jit(solution)/shard_map/mul | solution.py:14
  267.4 24.4 %copy.9 = bf16[26,32,128,128]{3,1,2,0:T(8,128)(2,1)} copy(bf16[26,32,128,128]{3,2,1,0:T(8,128)(2,1)} %bitcast.49) | data formatting | bytes 54525952 | tf_op jit(solution)/shard_map/reshape | solution.py:17
  291.7 59.9 %all-reduce.5.cloned.1.call-done = (bf16[512,3328]{0,1:T(8,128)(2,1)}, bf16[512,3328]{0,1:T(8,128)(2,1)}) async-done(((bf16[512,3328]{0,1:T(8,128)(2,1)}, bf16[512,3328]{0,1:T(8,128)(2,1)}), (bf16[512,3328]{0,1:T(8,128)(2,1)}, bf16[512,3328]{0,1:T(8,128)(2,1)})) %all-reduce.5.cloned.1.call-update) | async-done | bytes 6815760 | tf_op jit(solution)/shard_map/psum | solution.py:30
  351.7 26.2 %fusion.20 = bf16[512,4096]{1,0:T(8,128)(2,1)} fusion(bf16[416,8,32,128]{3,2,1,0:T(8,128)(2,1)} %bitcast.54, bf16[512,3328]{0,1:T(8,128)(2,1)} %get-tuple-element.6, bf16[512,3328]{0,1:T(8,128)(2,1)} %get-tuple-element.7), kind=kOutput, calls=%fused_computation.24 | convolution fusion | flops 13974372352 | bytes 38273024 | tf_op jit(solution)/shard_map/dot_general | solution.py:33
  377.8 0.0 reduce-scatter.2.cloned.1.call-update
  377.9 88.9 %reduce-scatter.2.cloned.1.call-done = bf16[64,4096]{1,0:T(8,128)(2,1)} async-done(((bf16[512,4096]{1,0:T(8,128)(2,1)}), bf16[64,4096]{1,0:T(8,128)(2,1)}) %reduce-scatter.2.cloned.1.call-update) | async-done | bytes 524304 | tf_op jit(solution)/shard_map/reduce_scatter | solution.py:34
  (10 shorter events, 0.1 us)
Async XLA Ops:
  6.5 166.0 %all-gather.2.cloned.1.call-start = ((), (), s32[]{:S(2)}) async-start(), calls=%async_computation.1 | async-start | bytes 4718592 | tf_op jit(solution)/shard_map/all_gather | solution.py:25
  7.3 344.4 %all-reduce.5.cloned.1.call-start = ((), (), s32[]{:S(2)}) async-start(), calls=%async_computation.3 | async-start | bytes 13631488 | tf_op jit(solution)/shard_map/psum | solution.py:30
  136.6 35.4 %copy-start = (s32[26,32]{1,0:T(8,128)S(1)}, s32[26,32]{1,0:T(8,128)}, u32[]{:S(2)}) copy-start(s32[26,32]{1,0:T(8,128)} %param.13) | copy-start | bytes 9988
  221.5 245.2 %reduce-scatter.2.cloned.1.call-start = ((), (), s32[]{:S(2)}) async-start(), calls=%async_computation.2 | async-start | bytes 4718592 | tf_op jit(solution)/shard_map/reduce_scatter | solution.py:34
Sparse Core Ops, SparseCore 0:
  9.5 76.0 all-gather.1
  221.6 130.0 all-reduce.4
  378.0 88.6 reduce-scatter.1
where the time goes:
time: 481 us; the launch traced here: 474 us
  local copies, waits for them, and re-layouts  180 us (37%)
  waiting for transfers between devices  150 us (31%)
  matrix products  75.1 us (16%)
  other arithmetic  55.8 us (12%)
  between operations  13.6 us (3%)
    reshape x3, local copies, waits for them, and re-layouts, dense_tile(): picked.reshape(in_blocks, out_blocks, block, block).transpose(0, 2, 1, 3)  94.7 us
    reduce_scatter x1, waiting for transfers between devices, local(): lax.psum_scatter(partial_out.astype(jnp.bfloat16), 'col', scatter_dimensi...  88.9 us
    gather x3, local copies, waits for them, and re-layouts, dense_tile(): jnp.take(packed_tile, slot_index, axis=0)  83.6 us
    psum x1, waiting for transfers between devices, local(): lax.psum(up_rows.astype(jnp.bfloat16), 'row').astype(jnp.float32)  59.9 us
    mul x2, other arithmetic, dense_tile(): jnp.take(packed_tile, slot_index, axis=0)  55 us
    dot_general x1, matrix products, local(): jnp.dot(every_hidden, down_dense, preferred_element_type=jnp.float32)  26.2 us
    dot_general x1, matrix products, local(): gate_rows = jnp.dot(segment, gate_dense, preferred_element_type=jnp.float32)  24.5 us
    dot_general x1, matrix products, local(): up_rows = jnp.dot(segment, up_dense, preferred_element_type=jnp.float32)  24.4 us
  transfers between devices with their start and end apart: 3, of which 2 were waited for; matrix products, arithmetic and copies ran while one was open for 50% of the time, Pallas kernels for 0%

commit v1 on v0

v1 whole, which is shorter than its diff:
```python
import functools

import jax
import jax.numpy as jnp
from jax import lax
from jax.experimental import pallas as pl
from jax.experimental.pallas import tpu as pltpu
from jax.sharding import PartitionSpec as P


def slot_tables(keep, cap):
    rows, cols = keep.shape
    flat = keep.reshape(-1).astype(jnp.int32)
    slot = (jnp.cumsum(flat) - flat).reshape(rows, cols)
    base = jnp.minimum(slot[:, 0], cap - cols)
    index = jnp.where(keep == 1, slot - base[:, None], -1)
    return base.astype(jnp.int32), index.reshape(-1).astype(jnp.int32)


def sparse_kernel(base_ref, index_ref, x_ref, *refs, n_w, cols, block):
    w_refs = refs[:n_w]
    o_refs = refs[n_w:2 * n_w]
    acc_refs = refs[2 * n_w:]
    r = pl.program_id(0)

    @pl.when(r == 0)
    def _():
        for acc in acc_refs:
            acc[...] = jnp.zeros(acc.shape, acc.dtype)

    for c in range(cols):
        k = index_ref[r * cols + c]

        @pl.when(k >= 0)
        def _():
            x = x_ref[...]
            for w, acc in zip(w_refs, acc_refs):
                acc[c] += jnp.dot(x, w[k], preferred_element_type=jnp.float32)

    @pl.when(r == pl.num_programs(0) - 1)
    def _():
        for o, acc in zip(o_refs, acc_refs):
            for c in range(cols):
                o[:, c * block:(c + 1) * block] = acc[c].astype(o.dtype)


def sparse_matmul(x, packed, keep):
    rows, cols = keep.shape
    cap, block, _ = packed[0].shape
    t = x.shape[0]
    n_w = len(packed)
    base, index = slot_tables(keep, cap)
    w_spec = pl.BlockSpec((pl.Element(cols), pl.Element(block), pl.Element(block)), lambda r, b, i: (b[r], 0, 0))
    kernel = functools.partial(sparse_kernel, n_w=n_w, cols=cols, block=block)
    flops = 2 * t * block * block * rows * cols * n_w
    bytes_accessed = x.size * 2 + n_w * (cap * block * block * 2 + t * cols * block * 2)
    return pl.pallas_call(
        kernel,
        grid_spec=pltpu.PrefetchScalarGridSpec(
            num_scalar_prefetch=2,
            grid=(rows,),
            in_specs=[pl.BlockSpec((t, block), lambda r, b, i: (0, r))] + [w_spec] * n_w,
            out_specs=[pl.BlockSpec((t, cols * block), lambda r, b, i: (0, 0))] * n_w,
            scratch_shapes=[pltpu.VMEM((cols, t, block), jnp.float32)] * n_w,
        ),
        out_shape=[jax.ShapeDtypeStruct((t, cols * block), jnp.bfloat16)] * n_w,
        compiler_params=pltpu.CompilerParams(dimension_semantics=("arbitrary",)),
        cost_estimate=pl.CostEstimate(flops=flops, transcendentals=0, bytes_accessed=bytes_accessed),
    )(base, index, x, *packed)


def local(tokens, gate_packed, up_packed, down_packed, gate_keep, down_keep):
    segment = lax.all_gather(tokens, "col", axis=0, tiled=True)
    gate_rows, up_rows = sparse_matmul(segment, [gate_packed, up_packed], gate_keep)
    gate_sum, up_sum = (
        lax.psum(gate_rows, "row").astype(jnp.float32),
        lax.psum(up_rows, "row").astype(jnp.float32),
    )
    every_hidden = (jax.nn.silu(gate_sum) * up_sum).astype(jnp.bfloat16)
    (partial_out,) = sparse_matmul(every_hidden, [down_packed], down_keep)
    summed = lax.psum_scatter(partial_out, "col", scatter_dimension=0, tiled=True)
    return summed


def solution(mesh):
    in_specs = (
        P("col", "row"),
        P("row", "col", None),
        P("row", "col", None),
        P("col", "row", None),
        P("row", "col"),
        P("col", "row"),
    )
    out_specs = P("col", "row")
    return jax.shard_map(local, mesh=mesh, in_specs=in_specs, out_specs=out_specs, check_vma=False)
```

time: 481 us -> 580 us (1.21); the launches traced: 474 us -> 579 us
  waiting for transfers between devices: 150 us -> 393 us
  local copies, waits for them, and re-layouts: 180 us -> 3.62 us
  Pallas kernels: 0 us -> 162 us
  matrix products: 75.1 us -> 0 us
  other arithmetic: 55.8 us -> 7.77 us
    pallas_call x0 -> x2, Pallas kernels: none -> 162 us  [sparse_matmul(): pl.pallas_call(kernel, grid_spec=pltpu.PrefetchScalarGridSpec(num_scalar_...]
    psum x1, waiting for transfers between devices: 59.9 us -> 199 us  [local(): lax.psum(up_rows, 'row').astype(jnp.float32)]
    reshape x6 -> x5, local copies, waits for them, and re-layouts: 95.6 us -> 2.26 us  [the longest x2 1.36 us: slot_tables(): return (base.astype(jnp.int32), index.reshape(-1).astype(jnp.int32))]
    gather x3 -> x0, local copies, waits for them, and re-layouts: 83.6 us -> none  [dense_tile(): jnp.take(packed_tile, slot_index, axis=0)]
    dot_general x3 -> x0, matrix products: 75.1 us -> none  [the longest x1 26.2 us: local(): jnp.dot(every_hidden, down_dense, preferred_element_type=jnp.float32)]
    all_gather x1, waiting for transfers between devices: 0.01 us -> 74.5 us  [local(): segment = lax.all_gather(tokens, 'col', axis=0, tiled=True)]
    mul x2 -> x0, other arithmetic: 55 us -> none  [dense_tile(): jnp.take(packed_tile, slot_index, axis=0)]
    reduce_scatter x1, waiting for transfers between devices: 88.9 us -> 119 us  [local(): lax.psum_scatter(partial_out, 'col', scatter_dimension=0, tiled=True)]
  transfers between devices with their start and end apart: 3 -> 3, of which waited for: 2 -> 3; matrix products, arithmetic and copies ran while one was open for 50% -> 1% of each run, Pallas kernels for 0% -> 0%
where the time goes in v1:
time: 580 us; the launch traced here: 579 us
  waiting for transfers between devices  393 us (68%)
  Pallas kernels  162 us (28%)
  between operations  13.2 us (2%)
  other arithmetic  7.77 us (1%)
    psum x1, waiting for transfers between devices, local(): lax.psum(up_rows, 'row').astype(jnp.float32)  199 us
    pallas_call x2, Pallas kernels, sparse_matmul(): pl.pallas_call(kernel, grid_spec=pltpu.PrefetchScalarGridSpec(num_scalar_...  162 us
    reduce_scatter x1, waiting for transfers between devices, local(): lax.psum_scatter(partial_out, 'col', scatter_dimension=0, tiled=True)  119 us
    all_gather x1, waiting for transfers between devices, local(): segment = lax.all_gather(tokens, 'col', axis=0, tiled=True)  74.5 us
  transfers between devices with their start and end apart: 3, of which 3 were waited for; matrix products, arithmetic and copies ran while one was open for 1% of the time, Pallas kernels for 0%

profile of v1, /device:TPU:0, one launch (start us, length us, event | category | flops | bytes accessed | tf_op | source)
XLA Modules:
  0.0 579.4 jit_solution(15342811720146558002)
XLA Ops:
  6.5 0.0 all-gather.2.cloned.1.call-start
  6.5 0.7 all-gather.2.cloned.1.call-update
  7.3 0.0 all-reduce.5.cloned.1.call-start
  7.3 0.8 reshape.64
  8.1 0.3 reduce-window.24
  8.4 0.1 slice.33
  8.5 0.1 slice_reduce_fusion
  8.6 0.1 add_bitcast_fusion
  8.7 0.1 reshape.67
  8.8 0.7 sub.27
  9.5 0.1 fusion.5.base_ref
  9.7 0.0 copy-start.2
  9.7 0.8 subtract_select_fusion
  10.5 0.7 reshape.68.index_ref
  11.2 74.5 %all-gather.2.cloned.1.call-done.x_ref = bf16[512,4096]{1,0:T(8,128)(2,1)} async-done(((bf16[64,4096]{1,0:T(8,128)(2,1)}), bf16[512,4096]{1,0:T(8,128)(2,1)}) %all-gather.2.cloned.1.call-update) | async-done | bytes 4194320 | tf_op jit(solution)/shard_map/all_gather | solution.py:73
  85.6 0.0 copy-done.2
  85.6 72.5 %shard_map.64 = (bf16[512,3328]{1,0:T(8,128)(2,1)}, bf16[512,3328]{1,0:T(8,128)(2,1)}) custom-call(s32[32]{0:T(128)} %copy-done.2, s32[832]{0:T(1024)} %reshape.68.index_ref, bf16[512,4096]{1,0:T(8,128)(2,1)} %all-gather.2.cloned.1.call-done.x_ref, bf16[640,128,128]{2,1,0:T(8,128)(2,1)} %refs_0_.2, bf16[640,128,128]{2,1,0:T(8,128)(2,1)} %refs_1_.1), custom_call_target="tpu_custom_call" | custom-call | flops 27917287424 | bytes 52953088 | tf_op jit(solution)/shard_map/pallas_call | solution.py:57
  158.1 0.0 copy-start
  158.1 0.0 all-reduce.5.cloned.1.call-update
  158.1 0.0 reduce-scatter.2.cloned.1.call-start
  158.2 0.6 copy-done
  158.8 0.1 reshape.58
  158.9 0.3 reduce-window.16
  159.2 0.1 reshape.60
  159.3 0.1 slice.29
  159.4 0.1 slice_reduce_fusion.1
  159.5 0.1 broadcast.27
  159.6 0.1 reshape.62
  159.6 0.1 fusion.7
  159.7 0.1 fusion.6.base_ref
  159.8 0.0 copy-start.1
  159.8 0.1 subtract_select_fusion.1
  159.9 0.7 reshape.63.index_ref
  160.6 198.7 %all-reduce.5.cloned.1.call-done = (bf16[512,3328]{1,0:T(8,128)(2,1)}, bf16[512,3328]{1,0:T(8,128)(2,1)}) async-done(((bf16[512,3328]{1,0:T(8,128)(2,1)}, bf16[512,3328]{1,0:T(8,128)(2,1)}), (bf16[512,3328]{1,0:T(8,128)(2,1)}, bf16[512,3328]{1,0:T(8,128)(2,1)})) %all-reduce.5.cloned.1.call-update) | async-done | bytes 6815760 | tf_op jit(solution)/shard_map/psum | solution.py:77
  359.3 5.2 fusion.4.x_ref
  364.5 0.0 copy-done.1
  364.5 89.0 %shard_map.65 = bf16[512,4096]{1,0:T(8,128)(2,1)} custom-call(s32[26]{0:T(128)} %copy-done.1, s32[832]{0:T(1024)} %reshape.63.index_ref, bf16[512,3328]{1,0:T(8,128)(2,1)} %fusion.4.x_ref, bf16[640,128,128]{2,1,0:T(8,128)(2,1)} %refs_0_.3), custom_call_target="tpu_custom_call" | custom-call | flops 13958643712 | bytes 28573696 | tf_op jit(solution)/shard_map/pallas_call | solution.py:57
  453.5 0.0 reduce-scatter.2.cloned.1.call-update
  453.6 119.3 %reduce-scatter.2.cloned.1.call-done = bf16[64,4096]{1,0:T(8,128)(2,1)} async-done(((bf16[512,4096]{1,0:T(8,128)(2,1)}), bf16[64,4096]{1,0:T(8,128)(2,1)}) %reduce-scatter.2.cloned.1.call-update) | async-done | bytes 524304 | tf_op jit(solution)/shard_map/reduce_scatter | solution.py:81
  (4 shorter events, 0.1 us)
Async XLA Ops:
  6.5 79.1 %all-gather.2.cloned.1.call-start = ((), (), s32[]{:S(2)}) async-start(), calls=%async_computation.1 | async-start | bytes 4718592 | tf_op jit(solution)/shard_map/all_gather | solution.py:73
  7.3 352.1 %all-reduce.5.cloned.1.call-start = ((), (), s32[]{:S(2)}) async-start(), calls=%async_computation.3 | async-start | bytes 13631488 | tf_op jit(solution)/shard_map/psum | solution.py:77
  9.7 76.0 %copy-start.2 = (s32[32]{0:T(128)}, s32[32]{0:T(128)S(1)}, u32[]{:S(2)}) copy-start(s32[32]{0:T(128)S(1)} %fusion.5.base_ref) | copy-start | bytes 388
  158.1 0.7 copy-start
  158.1 414.7 %reduce-scatter.2.cloned.1.call-start = ((), (), s32[]{:S(2)}) async-start(), calls=%async_computation.2 | async-start | bytes 4718592 | tf_op jit(solution)/shard_map/reduce_scatter | solution.py:81
  159.8 204.7 %copy-start.1 = (s32[26]{0:T(128)}, s32[26]{0:T(128)S(1)}, u32[]{:S(2)}) copy-start(s32[26]{0:T(128)S(1)} %fusion.6.base_ref) | copy-start | bytes 316
Sparse Core Ops, SparseCore 0:
  9.5 76.0 all-gather.1
  158.3 200.9 all-reduce.4
  453.7 119.1 reduce-scatter.1
